TPU v7x, 256 devices: a whole 4x4x8 slice. The times are simulated.
256 devices in a mesh: row: 8 (over y, core), col: 32 (over x, z).
Axes of the slice: x: 4, y: 4, z: 8, core: 2. Of those that a mesh axis runs over, the one named last changes fastest.
Arguments:
- trailing_adjoint: float32 [12288, 12288], P('row', 'col'), may hold values from -3 to 3, as said below
- panel: float32 [12288, 256], P(('row', 'col')), may hold values from -0.0546875 to 0.0546875
- panel_adjoint: float32 [12288, 256], P(('row', 'col')), may hold values from -6 to 6
- diag_factor: float32 [256, 256], replicated, may hold values from -1 to 2, as said below
- diag_adjoint: float32 [256, 256], P('row', 'col'), may hold values from -6 to 6
Outputs:
- off_adjoint: float32 [12288, 256], P(('row', 'col'))
- block_adjoint: float32 [256, 256], replicated
Inputs may be any that keep to these rules, and one draw needn't show every extreme that they name: `trailing_adjoint`: symmetric. `diag_factor`: lower triangular with diagonal entries from 1 to 2.
All inputs are finite; a program needn't handle non-finite values.
Results may differ from a plain program's by a relative error of at most 0.000071.
Values sent between devices are 32-bit elements; how exact they have to be, the bound alone decides.
No kernel may reach another device: no remote copies, remote signals or barrier semaphores. Data moves between devices by JAX's collectives and lax.ppermute only.
A program may use at most 64 MiB of HBM per device.

v0:
```python
import jax
import jax.numpy as jnp
from jax import lax
from jax.sharding import PartitionSpec as P


def right_solve(factor, rows):
    return jax.scipy.linalg.solve_triangular(factor, rows.T, lower=True, trans=1).T


def left_solve(factor, matrix):
    return jax.scipy.linalg.solve_triangular(factor, matrix, lower=True, trans=1)


def diagonal_adjoint(factor, adjoint):
    product = jnp.dot(
        factor.T, adjoint, precision=lax.Precision.HIGHEST, preferred_element_type=jnp.float32
    )
    lower = jnp.tril(product) - 0.5 * jnp.diag(jnp.diag(product))
    symmetric = lower + lower.T
    half = left_solve(factor, symmetric)
    return 0.5 * left_solve(factor, half.T).T


def body(trailing_adjoint, panel, panel_adjoint, diag_factor, diag_adjoint):
    nrows = lax.axis_size("row")
    stretch = panel.shape[0]
    span = stretch * nrows
    col_index = lax.axis_index("col")
    gathered = lax.all_gather(panel, ("row", "col"), axis=0, tiled=True)
    column_rows = lax.dynamic_slice_in_dim(gathered, col_index * span, span, 0)
    product = lax.psum_scatter(
        jnp.dot(
            trailing_adjoint,
            column_rows,
            precision=lax.Precision.HIGHEST,
            preferred_element_type=jnp.float32,
        ),
        "col",
        scatter_dimension=0,
        tiled=True,
    )
    updated = panel_adjoint - 2.0 * product
    off_adjoint = right_solve(diag_factor, updated)
    local_term = jnp.dot(
        off_adjoint.T, panel, precision=lax.Precision.HIGHEST, preferred_element_type=jnp.float32
    )
    row_piece = lax.all_gather(diag_adjoint, "col", axis=1, tiled=True)
    full_adjoint = lax.all_gather(row_piece, "row", axis=0, tiled=True)
    total = lax.psum(local_term, ("row", "col"))
    accumulated = full_adjoint - total
    return (off_adjoint, diagonal_adjoint(diag_factor, accumulated))


def solution(mesh):
    return jax.shard_map(
        body,
        mesh=mesh,
        in_specs=(
            P("row", "col"),
            P(("row", "col"), None),
            P(("row", "col"), None),
            P(),
            P("row", "col"),
        ),
        out_specs=(P(("row", "col"), None), P()),
        check_vma=False,
    )
```

profile of v0, /device:TPU:2, one launch (start us, length us, event | category | flops | bytes accessed | tf_op | source)
XLA Modules:
  0.0 632.7 jit_solution(16761037603501634626)
XLA Ops:
  7.2 0.7 all-gather.2.cloned.1.call-update
  8.0 127.5 %all-gather.2.cloned.1.call-done = f32[12288,256]{1,0:T(8,128)} async-done(((f32[48,256]{1,0:T(8,128)}), f32[12288,256]{1,0:T(8,128)}) %all-gather.2.cloned.1.call-update) | async-done | bytes 12582928 | tf_op jit(solution)/shard_map/all_gather | solution.py:30
  135.4 6.2 convolution_bitcast_fusion
  141.6 3.1 copy.24
  144.8 41.9 %all_gather.10 = f32[32,256]{0,1:T(8,128)S(1)} all-gather(f32[32,8]{0,1:T(8,128)S(1)} %copy-done.4), channel_id=1, replica_groups=mesh['row'=8,'col'=32] {'col'}, dimensions={1}, use_global_device_ids=true | all-gather | bytes 33792 | tf_op jit(solution)/shard_map/all_gather | solution.py:48
  186.9 4.1 while.5
  186.9 0.6 fusion.32
  187.5 1.4 bitcast_dynamic-update-slice_fusion.2
  188.9 0.6 fusion.32
  189.5 1.4 bitcast_dynamic-update-slice_fusion.2
  191.0 19.7 %custom-call.7 = f32[2,128,128]{1,2,0:T(8,128)S(1)} custom-call(f32[2,128,128]{2,1,0:T(8,128)S(1)} %get-tuple-element.18), custom_call_target="InvertDiagBlocksLowerTriangular" | custom-call | tf_op jit(solution)/shard_map/jit(_solve_triangular)/triangular_solve | solution.py:8
  210.7 12.8 %all_gather.11 = f32[256,256]{1,0:T(8,128)S(1)} all-gather(f32[32,256]{1,0:T(8,128)S(1)} %copy.19), channel_id=1, replica_groups=mesh['row'=8,'col'=32] {'row'}, dimensions={0}, use_global_device_ids=true | all-gather | bytes 294912 | tf_op jit(solution)/shard_map/all_gather | solution.py:49
  223.5 136.2 %reduce-scatter.4.cloned.1.call-done = f32[48,256]{1,0:T(8,128)} async-done(((f32[1536,256]{1,0:T(8,128)}), f32[48,256]{1,0:T(8,128)}) %reduce-scatter.4.cloned.1.call-update) | async-done | bytes 49168 | tf_op jit(solution)/shard_map/reduce_scatter | solution.py:32
  359.7 0.8 subtract_bitcast_fusion
  361.2 1.1 fusion.16
  362.4 0.6 fusion.17
  363.0 256.3 %all-reduce.2.cloned.1.call-done = f32[256,256]{1,0:T(8,128)} async-done(((f32[256,256]{1,0:T(8,128)}), f32[256,256]{1,0:T(8,128)}) %all-reduce.2.cloned.1.call-update) | async-done | bytes 262160 | tf_op jit(solution)/shard_map/psum | solution.py:50
  619.3 1.6 fusion.2
  621.0 2.3 gather_fusion
  623.7 0.3 convolution_subtract_fusion.1
  624.4 0.3 fusion.5
  624.6 0.4 convolution_subtract_fusion
  625.0 0.3 fusion.10
  625.3 0.8 copy.22
  (32 shorter events, 1.8 us)
Async XLA Ops:
  7.2 128.3 %copy-start = (f32[1536,384]{1,0:T(8,128)S(1)}, f32[1536,384]{1,0:T(8,128)}, u32[]{:S(2)}) copy-start(f32[1536,384]{1,0:T(8,128)} %param.7) | copy-start | bytes 7077892
  7.2 128.2 %all-gather.2.cloned.1.call-start = ((), (), s32[]{:S(2)}) async-start(), calls=%async_computation.1 | async-start | bytes 12632064 | tf_op jit(solution)/shard_map/all_gather | solution.py:30
  7.9 351.8 %reduce-scatter.4.cloned.1.call-start = ((), (), s32[]{:S(2)}) async-start(), calls=%async_computation.3 | async-start | bytes 1622016 | tf_op jit(solution)/shard_map/reduce_scatter | solution.py:32
  141.6 3.2 copy-start.4
  141.6 45.1 %copy-start.1 = (f32[256,256]{1,0:T(8,128)S(1)}, f32[256,256]{1,0:T(8,128)}, u32[]{:S(2)}) copy-start(f32[256,256]{1,0:T(8,128)} %param.10) | copy-start | bytes 786436
  144.7 215.1 %copy-start.3 = (f32[48,256]{1,0:T(8,128)S(1)}, f32[48,256]{1,0:T(8,128)}, u32[]{:S(2)}) copy-start(f32[48,256]{1,0:T(8,128)} %param.9) | copy-start | bytes 147460
  144.7 216.5 %copy-start.2 = (f32[48,256]{1,0:T(8,128)S(1)}, f32[48,256]{1,0:T(8,128)}, u32[]{:S(2)}) copy-start(f32[48,256]{1,0:T(8,128)} %param.8) | copy-start | bytes 147460
  144.7 474.6 %all-reduce.2.cloned.1.call-start = ((), (), s32[]{:S(2)}) async-start(), calls=%async_computation.2 | async-start | bytes 524288 | tf_op jit(solution)/shard_map/psum | solution.py:50
Sparse Core Ops, SparseCore 0:
  11.8 123.5 all-gather.1
  144.8 214.8 reduce-scatter.3
  365.8 253.4 all-reduce.1
where the time goes:
time: 633 us
  waiting for transfers between devices  521 us (82%)
  blocking collectives  54.7 us (9%)
  other arithmetic  21.3 us (3%)
  between operations  13.9 us (2%)
  matrix products  11.2 us (2%)
  local copies, waits for them, and re-layouts  10.6 us (2%)
    psum x1, waiting for transfers between devices, body(): total = lax.psum(local_term, ('row', 'col'))  256 us
    reduce_scatter x1, waiting for transfers between devices, body(): lax.psum_scatter(jnp.dot(trailing_adjoint, column_rows, precision=lax.Pre...  136 us
    all_gather x1, waiting for transfers between devices, body(): gathered = lax.all_gather(panel, ('row', 'col'), axis=0, tiled=True)  127 us
    all_gather x1, blocking collectives, body(): row_piece = lax.all_gather(diag_adjoint, 'col', axis=1, tiled=True)  41.9 us
    another operation x3, other arithmetic, right_solve(): jax.scipy.linalg.solve_triangular(factor, rows.T, lower=True, trans=1)  19.7 us
    all_gather x1, blocking collectives, body(): full_adjoint = lax.all_gather(row_piece, 'row', axis=0, tiled=True)  12.8 us
  transfers between devices with their start and end apart: 3, of which 3 were waited for; matrix products, arithmetic and copies ran while one was open for 4% of the time, Pallas kernels for 0%

commit v1 on v0

--- a/solution.py
+++ b/solution.py
@@ -2,6 +2,13 @@
 import jax.numpy as jnp
 from jax import lax
 from jax.sharding import PartitionSpec as P
+
+
+def gather_over(array, name, dim):
+    size = lax.axis_size(name)
+    pieces = jnp.stack([array for _ in range(size)])
+    pieces = lax.all_to_all(pieces, name, split_axis=0, concat_axis=0)
+    return jnp.concatenate(pieces, axis=dim)
 
 
 def right_solve(factor, rows):
@@ -27,7 +34,7 @@
     stretch = panel.shape[0]
     span = stretch * nrows
     col_index = lax.axis_index("col")
-    gathered = lax.all_gather(panel, ("row", "col"), axis=0, tiled=True)
+    gathered = gather_over(panel, ("row", "col"), 0)
     column_rows = lax.dynamic_slice_in_dim(gathered, col_index * span, span, 0)
     product = lax.psum_scatter(
         jnp.dot(

time: 633 us -> 802 us (1.27)
  waiting for transfers between devices: 521 us -> 667 us
  starting transfers between devices: 0.12 us -> 15.6 us
    all_to_all x0 -> x1, waiting for transfers between devices: none -> 275 us  [gather_over(): pieces = lax.all_to_all(pieces, name, split_axis=0, concat_axis=0)]
    all_gather x1 -> x0, waiting for transfers between devices: 127 us -> none  [body(): gathered = lax.all_gather(panel, ('row', 'col'), axis=0, tiled=True)]
    all_to_all x0 -> x1, starting transfers between devices: none -> 15.6 us  [gather_over(): pieces = lax.all_to_all(pieces, name, split_axis=0, concat_axis=0)]
  transfers between devices with their start and end apart: 3 -> 3, of which waited for: 3 -> 3; matrix products, arithmetic and copies ran while one was open for 4% -> 3% of each run, Pallas kernels for 0% -> 0%
where the time goes in v1:
time: 802 us
  waiting for transfers between devices  667 us (83%)
  blocking collectives  54.8 us (7%)
  other arithmetic  21.3 us (3%)
  local copies, waits for them, and re-layouts  17.5 us (2%)
  starting transfers between devices  15.6 us (2%)
  between operations  14.2 us (2%)
  matrix products  11.3 us (1%)
    all_to_all x1, waiting for transfers between devices, gather_over(): pieces = lax.all_to_all(pieces, name, split_axis=0, concat_axis=0)  275 us
    psum x1, waiting for transfers between devices, body(): total = lax.psum(local_term, ('row', 'col'))  256 us
    reduce_scatter x1, waiting for transfers between devices, body(): lax.psum_scatter(jnp.dot(trailing_adjoint, column_rows, precision=lax.Pre...  136 us
    all_gather x1, blocking collectives, body(): row_piece = lax.all_gather(diag_adjoint, 'col', axis=1, tiled=True)  41.8 us
    another operation x3, other arithmetic, right_solve(): jax.scipy.linalg.solve_triangular(factor, rows.T, lower=True, trans=1)  19.7 us
  transfers between devices with their start and end apart: 3, of which 3 were waited for; matrix products, arithmetic and copies ran while one was open for 3% of the time, Pallas kernels for 0%

profile of v1, /device:TPU:2, one launch (start us, length us, event | category | flops | bytes accessed | tf_op | source)
XLA Modules:
  0.0 801.6 jit_solution(3201606763346870750)
XLA Ops:
  7.2 7.0 stack.2
  14.2 15.6 %all-to-all-start = ((f32[256,48,256]{2,1,0:T(8,128)}), f32[256,48,256]{2,1,0:T(8,128)}, u32[]{:S(2)}, u32[]{:S(2)}) async-start(f32[256,48,256]{2,1,0:T(8,128)} %stack.2), calls=%async_computation | async-start | bytes 25165824 | tf_op jit(solution)/shard_map/all_to_all | solution.py:10
  29.8 274.8 %all-to-all-done = f32[256,48,256]{2,1,0:T(8,128)} async-done(((f32[256,48,256]{2,1,0:T(8,128)}), f32[256,48,256]{2,1,0:T(8,128)}, u32[]{:S(2)}, u32[]{:S(2)}) %all-to-all-start) | async-done | bytes 12582944 | tf_op jit(solution)/shard_map/all_to_all | solution.py:10
  304.6 6.2 convolution_bitcast_fusion
  310.8 3.1 copy.24
  314.1 4.0 while.5
  314.1 0.6 fusion.32
  314.7 1.4 bitcast_dynamic-update-slice_fusion.2
  316.1 0.6 fusion.32
  316.7 1.4 bitcast_dynamic-update-slice_fusion.2
  318.0 19.7 %custom-call.7 = f32[2,128,128]{1,2,0:T(8,128)S(1)} custom-call(f32[2,128,128]{2,1,0:T(8,128)S(1)} %get-tuple-element.18), custom_call_target="InvertDiagBlocksLowerTriangular" | custom-call | tf_op jit(solution)/shard_map/jit(_solve_triangular)/triangular_solve | solution.py:15
  337.7 41.8 %all_gather.6 = f32[32,256]{0,1:T(8,128)S(1)} all-gather(f32[32,8]{0,1:T(8,128)S(1)} %copy-done.3), channel_id=1, replica_groups=mesh['row'=8,'col'=32] {'col'}, dimensions={1}, use_global_device_ids=true | all-gather | bytes 33792 | tf_op jit(solution)/shard_map/all_gather | solution.py:55
  379.6 13.0 %all_gather.7 = f32[256,256]{1,0:T(8,128)S(1)} all-gather(f32[32,256]{1,0:T(8,128)S(1)} %copy.19), channel_id=1, replica_groups=mesh['row'=8,'col'=32] {'row'}, dimensions={0}, use_global_device_ids=true | all-gather | bytes 294912 | tf_op jit(solution)/shard_map/all_gather | solution.py:56
  392.6 135.9 %reduce-scatter.4.cloned.1.call-done = f32[48,256]{1,0:T(8,128)} async-done(((f32[1536,256]{1,0:T(8,128)}), f32[48,256]{1,0:T(8,128)}) %reduce-scatter.4.cloned.1.call-update) | async-done | bytes 49168 | tf_op jit(solution)/shard_map/reduce_scatter | solution.py:39
  528.5 0.8 subtract_bitcast_fusion
  530.0 1.1 fusion.16
  531.2 0.6 fusion.17
  531.8 256.1 %all-reduce.2.cloned.1.call-done = f32[256,256]{1,0:T(8,128)} async-done(((f32[256,256]{1,0:T(8,128)}), f32[256,256]{1,0:T(8,128)}) %all-reduce.2.cloned.1.call-update) | async-done | bytes 262160 | tf_op jit(solution)/shard_map/psum | solution.py:57
  787.9 1.6 fusion.2
  789.6 2.3 gather_fusion
  792.3 0.3 convolution_subtract_fusion.1
  793.0 0.3 fusion.5
  793.3 0.4 convolution_subtract_fusion
  794.0 0.8 copy.22
  (30 shorter events, 2.0 us)
Async XLA Ops:
  7.2 297.5 %copy-start = (f32[1536,384]{1,0:T(8,128)S(1)}, f32[1536,384]{1,0:T(8,128)}, u32[]{:S(2)}) copy-start(f32[1536,384]{1,0:T(8,128)} %param.7) | copy-start | bytes 7077892
  14.2 290.4 %all-to-all-start = ((f32[256,48,256]{2,1,0:T(8,128)}), f32[256,48,256]{2,1,0:T(8,128)}, u32[]{:S(2)}, u32[]{:S(2)}) async-start(f32[256,48,256]{2,1,0:T(8,128)} %stack.2), calls=%async_computation | async-start | bytes 25165824 | tf_op jit(solution)/shard_map/all_to_all | solution.py:10
  29.8 498.7 %reduce-scatter.4.cloned.1.call-start = ((), (), s32[]{:S(2)}) async-start(), calls=%async_computation.3 | async-start | bytes 1622016 | tf_op jit(solution)/shard_map/reduce_scatter | solution.py:39
  310.8 3.2 copy-start.1
  310.8 26.9 %copy-start.3 = (f32[32,8]{0,1:T(8,128)S(1)}, f32[32,8]{0,1:T(8,128)}, u32[]{:S(2)}) copy-start(f32[32,8]{0,1:T(8,128)} %param.11) | copy-start | bytes 3076
  313.9 216.1 %copy-start.2 = (f32[48,256]{1,0:T(8,128)S(1)}, f32[48,256]{1,0:T(8,128)}, u32[]{:S(2)}) copy-start(f32[48,256]{1,0:T(8,128)} %param.8) | copy-start | bytes 147460
  313.9 474.0 %all-reduce.2.cloned.1.call-start = ((), (), s32[]{:S(2)}) async-start(), calls=%async_computation.2 | async-start | bytes 524288 | tf_op jit(solution)/shard_map/psum | solution.py:57
Sparse Core Ops, SparseCore 0:
  314.0 214.4 reduce-scatter.3
  534.5 253.3 all-reduce.1
